TPU v7x, 256 devices: a whole 4x4x8 slice. The times are simulated.
256 devices in a mesh: lat: 32 (over x_lo, z, core), lon: 8 (over y, x_hi).
Axes of the slice: x: 4 (x_hi: 2, x_lo: 2; x = x_hi * 2 + x_lo), y: 4, z: 8, core: 2. Of those that a mesh axis runs over, the one named last changes fastest.
Arguments:
- tokens: bfloat16 [4, 192, 96, 512], P(None, 'lat', 'lon'), may hold values from -6 to 6
- w_qkv: bfloat16 [512, 1536], P('lon'), may hold values from -0.25 to 0.25
- w_out: bfloat16 [512, 512], P('lon'), may hold values from -0.25 to 0.25
- gain: float32 [512], replicated, may hold values from 0.1 to 1.9
- tau: float32 [8], replicated, may hold values from 1 to 12
- cotangent: bfloat16 [4, 192, 96, 512], P(None, 'lat', 'lon'), may hold values from -6 to 6
Outputs:
- output: bfloat16 [4, 192, 96, 512], P(None, 'lat', 'lon')
- grad_tokens: bfloat16 [4, 192, 96, 512], P(None, 'lat', 'lon')
- grad_qkv: float32 [512, 1536], P('lon')
- grad_out: float32 [512, 512], P('lon')
All inputs are finite; a program needn't handle non-finite values.
Results may differ from a plain program's by a relative error of at most 0.035.
Values may be sent and summed in bfloat16 or wider, within the bound.
No kernel may reach another device: no remote copies, remote signals or barrier semaphores. Data moves between devices by JAX's collectives and lax.ppermute only.
A program may use at most 128 MiB of HBM per device.

v0:
```python
import jax
import jax.numpy as jnp
from jax import lax
from jax.sharding import PartitionSpec as P

LV = 4
WL = 2
WH = 6
WW = 12
KEYS = 288


NORM_EPS = 1e-05
UNIT_EPS = 1e-06


def with_halo(shard, sides, width, wrap):
    for axis, dim in sides:
        peers, length = (lax.axis_size(axis), shard.shape[dim])
        up = [(i, (i + 1) % peers) for i in range(peers if wrap else peers - 1)]
        down = [(j, i) for i, j in up]
        last = lax.slice_in_dim(shard, length - width, length, axis=dim)
        initial = lax.slice_in_dim(shard, 0, width, axis=dim)
        before = lax.ppermute(last, axis, up)
        after = lax.ppermute(initial, axis, down)
        shard = jnp.concatenate([before, shard, after], axis=dim)
    return shard


def from_behind(block, axis, distance):
    devices = range(lax.axis_size(axis))
    route = [((i - distance) % len(devices), i) for i in devices]
    return lax.ppermute(block, axis, route)


def from_behind_2(block, axis, distance):
    devices = range(lax.axis_size(axis))
    route = [(i - distance, i) for i in devices if i - distance in devices]
    return lax.ppermute(block, axis, route)


def unit_rows(vectors):
    scaling = lax.rsqrt(jnp.sum(vectors * vectors, axis=-1, keepdims=True) + UNIT_EPS)
    return (vectors * scaling, scaling)


def unit_back(vectors, scaling, gradient):
    inner_sum = jnp.sum(vectors * gradient, axis=-1, keepdims=True)
    return scaling * (gradient - vectors * (inner_sum * scaling * scaling))


def norm_forward(y_rows):
    centered = y_rows - jnp.mean(y_rows, axis=-1, keepdims=True)
    inverse = lax.rsqrt(jnp.mean(centered * centered, axis=-1, keepdims=True) + NORM_EPS)
    return (centered * inverse, inverse)


def norm_back(normed, inverse, upstream):
    mean_up = jnp.mean(upstream, axis=-1, keepdims=True)
    mean_cross = jnp.mean(upstream * normed, axis=-1, keepdims=True)
    return inverse * (upstream - mean_up - normed * mean_cross)


def key_windows(extended):
    ext_rows = extended.shape[1]
    ext_cols = extended.shape[2]
    channels = extended.shape[3]
    shaped = extended.reshape(LV, ext_rows // WH, WH, ext_cols // WW, WW, channels)
    return shaped.transpose(1, 3, 0, 2, 4, 5).reshape(
        ext_rows // WH, ext_cols // WW, KEYS, channels
    )


def key_layout(windows):
    win_rows = windows.shape[0]
    win_cols = windows.shape[1]
    channels = windows.shape[3]
    shaped = windows.reshape(win_rows, win_cols, LV, WH, WW, channels)
    return shaped.transpose(2, 0, 3, 1, 4, 5).reshape(LV, win_rows * WH, win_cols * WW, channels)


def query_units(own_grid):
    lat_rows = own_grid.shape[1]
    lon_cols = own_grid.shape[2]
    channels = own_grid.shape[3]
    half_h = WH // 2
    half_w = WW // 2
    shaped = own_grid.reshape(LV, lat_rows // half_h, half_h, lon_cols // half_w, half_w, channels)
    return shaped.transpose(1, 3, 0, 2, 4, 5).reshape(
        lat_rows // half_h, lon_cols // half_w, LV * half_h * half_w, channels
    )


def query_layout(units):
    row_units = units.shape[0]
    col_units = units.shape[1]
    channels = units.shape[3]
    half_h = WH // 2
    half_w = WW // 2
    shaped = units.reshape(row_units, col_units, LV, half_h, half_w, channels)
    return shaped.transpose(2, 0, 3, 1, 4, 5).reshape(
        LV, row_units * half_h, col_units * half_w, channels
    )


def spread_units(blocks, along):
    win_total = blocks.shape[along]
    first_part = lax.slice_in_dim(blocks, 0, 1, axis=along)
    middle_part = jnp.repeat(lax.slice_in_dim(blocks, 1, win_total - 1, axis=along), 2, axis=along)
    last_part = lax.slice_in_dim(blocks, win_total - 1, win_total, axis=along)
    return jnp.concatenate([first_part, middle_part, last_part], axis=along)


def merge_units(units, along):
    unit_total = units.shape[along]
    first_part = lax.slice_in_dim(units, 0, 1, axis=along)
    last_part = lax.slice_in_dim(units, unit_total - 1, unit_total, axis=along)
    middle = lax.slice_in_dim(units, 1, unit_total - 1, axis=along)
    new_shape = middle.shape[:along] + ((unit_total - 2) // 2, 2) + middle.shape[along + 1 :]
    middle_part = jnp.sum(middle.reshape(new_shape), axis=along + 1)
    return jnp.concatenate([first_part, middle_part, last_part], axis=along)


def cross_rows(left_mat, right_mat):
    return lax.dot_general(
        left_mat, right_mat, (((0,), (0,)), ((), ())), preferred_element_type=jnp.float32
    )


def on_device(tokens, w_qkv, w_out, gain, tau, cotangent):
    lat_rows = tokens.shape[1]
    lon_cols = tokens.shape[2]
    model_width = tokens.shape[3]
    head_count = tau.shape[0]
    head_dim = model_width // head_count
    tok_count = LV * lat_rows * lon_cols
    half_h = WH // 2
    half_w = WW // 2
    tok_flat = tokens.reshape(tok_count, model_width)
    src_count = tok_flat.shape[0]
    tok_part = tok_flat
    projected = jnp.dot(
        tok_part,
        lax.all_gather(w_qkv, "lon", axis=0, tiled=True),
        preferred_element_type=jnp.float32,
    )
    proj_b = projected.astype(jnp.bfloat16)
    query_grid = proj_b[:, :model_width].reshape(LV, lat_rows, lon_cols, model_width)
    query_f = query_grid.astype(jnp.float32).reshape(tok_count, head_count, head_dim)
    key_f = (
        proj_b[:, model_width : 2 * model_width]
        .astype(jnp.float32)
        .reshape(src_count, head_count, head_dim)
    )
    query_n, query_scale = unit_rows(query_f)
    key_n, key_scale = unit_rows(key_f)
    query_b = query_n.astype(jnp.bfloat16).reshape(LV, lat_rows, lon_cols, model_width)
    key_b = key_n.astype(jnp.bfloat16).reshape(src_count, model_width)
    kv_source = jnp.concatenate([key_b, proj_b[:, 2 * model_width :]], axis=1).reshape(
        LV, lat_rows, lon_cols, 2 * model_width
    )
    ext_rows = with_halo(kv_source, (("lat", 1),), half_h, False)
    ext_all = with_halo(ext_rows, (("lon", 2),), half_w, True)
    keys_units = spread_units(spread_units(key_windows(ext_all), 0), 1)
    row_units = keys_units.shape[0]
    col_units = keys_units.shape[1]
    key_u = keys_units[..., :model_width].reshape(row_units, col_units, KEYS, head_count, head_dim)
    value_u = keys_units[..., model_width:].reshape(
        row_units, col_units, KEYS, head_count, head_dim
    )
    query_count = LV * half_h * half_w
    query_u = query_units(query_b).reshape(row_units, col_units, query_count, head_count, head_dim)
    token_ids = jnp.arange(KEYS)
    query_ids = jnp.arange(query_count)
    key_level = (token_ids // (WH * WW) + WL // 2) // WL
    query_level = (query_ids // (half_h * half_w) + WL // 2) // WL
    same_level = query_level[:, None] == key_level[None, :]
    unit_ids = jnp.arange(row_units)
    ext_row = WH * ((unit_ids[:, None] + 1) // 2) + token_ids[None, :] // WW % WH
    global_row = lax.axis_index("lat") * lat_rows - half_h + ext_row
    inside = (global_row >= 0) & (global_row < lat_rows * lax.axis_size("lat"))
    allowed = (same_level[None, :, :] & inside[:, None, :]).astype(jnp.float32)[:, None, None]
    temper = tau[:, None, None]
    scores = (
        jnp.einsum("abqhd,abkhd->abhqk", query_u, key_u, preferred_element_type=jnp.float32)
        * temper
    )
    weights = jnp.exp(scores) * allowed
    probs = weights / jnp.sum(weights, axis=-1, keepdims=True)
    probs_b = probs.astype(jnp.bfloat16)
    mixed = jnp.einsum(
        "abhqk,abkhd->abqhd", probs_b, value_u, preferred_element_type=jnp.float32
    ).astype(jnp.bfloat16)
    attended = query_layout(mixed.reshape(row_units, col_units, query_count, model_width)).reshape(
        tok_count, model_width
    )
    att_part = attended
    y_rows = jnp.dot(
        att_part,
        lax.all_gather(w_out, "lon", axis=0, tiled=True),
        preferred_element_type=jnp.float32,
    )
    normed, inverse = norm_forward(y_rows)
    output = (tok_flat.astype(jnp.float32) + gain * normed).astype(jnp.bfloat16)
    cot_flat = cotangent.reshape(tok_count, model_width).astype(jnp.float32)
    grad_y = norm_back(normed, inverse, gain * cot_flat).astype(jnp.bfloat16)
    grad_att = jnp.dot(
        grad_y,
        lax.all_gather(w_out, "lon", axis=0, tiled=True).T,
        preferred_element_type=jnp.float32,
    )
    grad_att_b = grad_att.astype(jnp.bfloat16).reshape(LV, lat_rows, lon_cols, model_width)
    grad_u = query_units(grad_att_b).reshape(
        row_units, col_units, query_count, head_count, head_dim
    )
    dprob = jnp.einsum("abqhd,abkhd->abhqk", grad_u, value_u, preferred_element_type=jnp.float32)
    total_sum = jnp.sum(probs * dprob, axis=-1, keepdims=True)
    dscore = (temper * (probs * (dprob - total_sum))).astype(jnp.bfloat16)
    dquery = jnp.einsum("abhqk,abkhd->abqhd", dscore, key_u, preferred_element_type=jnp.float32)
    dkey = jnp.einsum("abhqk,abqhd->abkhd", dscore, query_u, preferred_element_type=jnp.float32)
    dvalue = jnp.einsum("abhqk,abqhd->abkhd", probs_b, grad_u, preferred_element_type=jnp.float32)
    key_grads = jnp.concatenate(
        [
            dkey.reshape(row_units, col_units, KEYS, model_width),
            dvalue.reshape(row_units, col_units, KEYS, model_width),
        ],
        axis=3,
    )
    ext_grad = key_layout(merge_units(merge_units(key_grads, 0), 1))
    dquery_own = query_layout(
        dquery.reshape(row_units, col_units, query_count, model_width)
    ).reshape(tok_count, head_count, head_dim)
    grad_q = unit_back(query_f, query_scale, dquery_own).reshape(
        LV, lat_rows, lon_cols, model_width
    )
    west_rim = ext_grad[:, :, :half_w]
    east_rim = ext_grad[:, :, half_w + lon_cols :]
    center = ext_grad[:, :, half_w : half_w + lon_cols]
    from_east = from_behind(west_rim.astype(jnp.bfloat16), "lon", -1).astype(west_rim.dtype)
    from_west = from_behind(east_rim.astype(jnp.bfloat16), "lon", 1).astype(east_rim.dtype)
    center = center.at[:, :, :half_w].add(from_west).at[:, :, lon_cols - half_w :].add(from_east)
    north_rim = center[:, :half_h]
    south_rim = center[:, half_h + lat_rows :]
    middle = center[:, half_h : half_h + lat_rows]
    from_south = from_behind_2(north_rim.astype(jnp.bfloat16), "lat", -1).astype(north_rim.dtype)
    from_north = from_behind_2(south_rim.astype(jnp.bfloat16), "lat", 1).astype(south_rim.dtype)
    middle = middle.at[:, :half_h].add(from_north).at[:, lat_rows - half_h :].add(from_south)
    own_grads = middle.reshape(tok_count, 2 * model_width)
    grad_k = unit_back(
        key_f, key_scale, own_grads[:, :model_width].reshape(tok_count, head_count, head_dim)
    ).reshape(tok_count, model_width)
    grad_q_src = grad_q.reshape(tok_count, model_width)
    dvalue_src = own_grads[:, model_width:]
    grad_proj = jnp.concatenate([grad_q_src, grad_k, dvalue_src], axis=1).astype(jnp.bfloat16)
    grad_in = jnp.dot(
        grad_proj,
        lax.all_gather(w_qkv, "lon", axis=0, tiled=True).T,
        preferred_element_type=jnp.float32,
    )
    grad_tokens = (
        (cot_flat + grad_in).astype(jnp.bfloat16).reshape(LV, lat_rows, lon_cols, model_width)
    )
    tok_part = tok_flat
    att_part = attended
    shard_sum = lax.psum_scatter(
        jnp.concatenate(
            [cross_rows(tok_part, grad_proj), cross_rows(att_part, grad_y)], axis=1
        ).astype(jnp.bfloat16),
        "lon",
        scatter_dimension=0,
        tiled=True,
    )
    summed = lax.psum(shard_sum, "lat").astype(jnp.float32)
    grad_qkv = summed[:, : 3 * model_width]
    grad_out = summed[:, 3 * model_width :]
    return (output.reshape(LV, lat_rows, lon_cols, model_width), grad_tokens, grad_qkv, grad_out)


def solution(mesh):
    in_specs = (
        P(None, "lat", "lon", None),
        P("lon", None),
        P("lon", None),
        P(),
        P(),
        P(None, "lat", "lon", None),
    )
    out_specs = (
        P(None, "lat", "lon", None),
        P(None, "lat", "lon", None),
        P("lon", None),
        P("lon", None),
    )
    return jax.shard_map(
        on_device, mesh=mesh, in_specs=in_specs, out_specs=out_specs, check_vma=False
    )
```

profile of v0, /device:TPU:1, one launch (start us, length us, event | category | flops | bytes accessed | tf_op | source)
XLA Modules:
  0.0 591.8 jit_solution(12265839422820028312)
XLA Ops:
  11.7 34.2 %all_gather.9 = bf16[512,512]{1,0:T(8,128)(2,1)} all-gather(bf16[64,512]{1,0:T(8,128)(2,1)} %param.16), channel_id=1, replica_groups=mesh['lat'=32,'lon'=8] {'lon'}, dimensions={0}, use_global_device_ids=true | all-gather | bytes 589824 | tf_op jit(solution)/shard_map/all_gather | solution.py:200
  46.0 24.0 %all-gather.2.cloned.1.call-done = bf16[512,1536]{1,0:T(8,128)(2,1)} async-done(((bf16[64,1536]{1,0:T(8,128)(2,1)}), bf16[512,1536]{1,0:T(8,128)(2,1)}) %all-gather.2.cloned.1.call-update) | async-done | bytes 1572880 | tf_op jit(solution)/shard_map/all_gather | solution.py:144
  70.0 2.0 convolution_convert_fusion.1
  75.5 4.1 collective-permute-start
  79.6 1.9 collective-permute-start.1
  84.9 4.2 collective-permute-done.1
  93.5 5.0 collective-permute-start.3
  100.9 1.5 fusion.34
  104.3 6.7 %collective-permute-done.2 = bf16[4,12,6,1024]{3,0,2,1:T(4,128)(2,1)} collective-permute-done((bf16[4,12,6,1024]{3,0,2,1:T(4,128)(2,1)}, bf16[4,12,6,1024]{3,0,2,1:T(4,128)(2,1)}, u32[]{:S(2)}, u32[]{:S(2)}) %collective-permute-start.2) | collective-permute-done | bytes 589856 | tf_op jit(solution)/shard_map/ppermute | solution.py:24
  112.3 4.8 collective-permute-done.3
  118.4 2.3 pad_maximum_fusion
  120.7 1.8 copy.106
  126.0 3.2 pad_maximum_fusion.3
  129.2 2.8 copy.113
  132.0 4.3 copy.109
  137.4 1.8 copy-done.12
  149.1 3.8 fusion.62
  152.9 2.8 convolution_bitcast_fusion
  155.7 16.7 %fusion.13 = f32[2,2,288,8,64]{2,4,3,1,0:T(8,128)} fusion(bf16[2,2,72,8,64]{2,4,3,1,0:T(8,128)(2,1)S(1)} %copy-done.17, f32[2,2,8,72,288]{4,3,2,1,0:T(8,128)} %fusion.62, f32[8]{0:T(128)S(1)} %copy-done.37, f32[2,2,8,72,288]{4,3,2,1,0:T(8,128)} %copy-done.12, f32[2,2,8,72]{3,2,1,0:T(8,128)S(1)} %get-tuple-element.86, f32[2,72,288]{2,1,0:T(8,128)S(1)} %copy-done.27), kind=kOutput, calls=%fused_computation.18 | convolution fusion | flops 92236320 | bytes 8137760 | tf_op jit(solution)/shard_map/abhqk,abqhd->abkhd/dot_general | solution.py:220
  172.4 5.5 copy.129
  177.9 4.1 concatenate.50
  182.1 5.5 copy.131
  187.6 5.6 concatenate.51
  193.2 4.2 maximum_bitcast_fusion
  197.4 3.1 copy.132
  202.8 1.6 fusion.56
  205.7 4.8 collective-permute-start.5
  210.5 18.4 %fusion.18 = f32[2,2,72,8,64]{2,4,3,1,0:T(8,128)} fusion(bf16[2,2,288,8,64]{2,4,3,1,0:T(8,128)(2,1)S(1)} %bitcast.80, f32[2,2,8,72,288]{4,3,2,1,0:T(8,128)} %fusion.62, f32[8]{0:T(128)S(1)} %copy-done.37, f32[2,2,8,72,288]{4,3,2,1,0:T(8,128)} %copy-done.12, f32[2,2,8,72]{3,2,1,0:T(8,128)S(1)} %get-tuple-element.86, f32[2,72,288]{2,1,0:T(8,128)} %and_convert_fusion), kind=kOutput, calls=%fused_computation.22 | convolution fusion | flops 92236320 | bytes 7253024 | tf_op jit(solution)/shard_map/abhqk,abkhd->abqhd/dot_general | solution.py:219
  229.0 2.6 slice.241
  231.5 2.7 copy.122
  234.3 2.5 reshape_reshape.30
  236.8 2.1 copy.123
  238.9 2.5 reshape_reshape.32
  241.4 2.6 copy.125
  244.0 2.2 convolution_convert_fusion.2
  246.2 1.9 fusion.25
  248.1 1.6 fusion.24
  251.3 7.6 %collective-permute-start.6 = (bf16[4,3,12,1024]{3,0,2,1:T(4,128)(2,1)}, bf16[4,3,12,1024]{3,0,2,1:T(4,128)(2,1)}, u32[]{:S(2)}, u32[]{:S(2)}) collective-permute-start(bf16[4,3,12,1024]{3,0,2,1:T(4,128)(2,1)} %get-tuple-element.77), channel_id=1, source_target_pairs={{0,8},{8,16},{16,24},{24,32},{32,40},{40,48},{48,56},{56,64},{64,7... | collective-permute-start | bytes 884744 | tf_op jit(solution)/shard_map/ppermute | solution.py:39
  259.1 1.9 collective-permute-start.7
  261.0 2.0 reshape_reshape.31
  265.5 1.7 collective-permute-done.7
  269.3 1.9 convert_multiply_fusion.1
  274.5 2.1 multiply_convert_fusion.2
  277.9 2.5 copy.141
  281.5 75.5 %reduce-scatter.4.cloned.1.call-done = bf16[64,2048]{1,0:T(8,128)(2,1)} async-done(((bf16[512,2048]{1,0:T(8,128)(2,1)}), bf16[64,2048]{1,0:T(8,128)(2,1)}) %reduce-scatter.4.cloned.1.call-update) | async-done | bytes 262160
  356.9 2.0 copy.142
  359.0 2.1 fusion.22
  362.0 220.1 %all-reduce.2.cloned.1.call-done = bf16[64,2048]{0,1:T(8,128)(2,1)} async-done(((bf16[64,2048]{0,1:T(8,128)(2,1)}), bf16[64,2048]{0,1:T(8,128)(2,1)}) %all-reduce.2.cloned.1.call-update) | async-done | bytes 262160 | tf_op jit(solution)/shard_map/psum | solution.py:273
  (182 shorter events, 55.9 us)
Async XLA Ops:
  7.2 62.8 %all-gather.2.cloned.1.call-start = ((), (), s32[]{:S(2)}) async-start(), calls=%async_computation.1 | async-start | bytes 1769472 | tf_op jit(solution)/shard_map/all_gather | solution.py:144
  7.9 349.0 %reduce-scatter.4.cloned.1.call-start = ((), (), s32[]{:S(2)}) async-start(), calls=%async_computation.3 | async-start | bytes 2359296
  9.1 62.9 %copy-start.21 = (bf16[288,512]{1,0:T(8,128)(2,1)}, bf16[288,512]{1,0:T(8,128)(2,1)S(1)}, u32[]{:S(2)}) copy-start(bf16[288,512]{1,0:T(8,128)(2,1)S(1)} %reshape.455) | copy-start | bytes 884740
  72.0 1.4 copy-start.9
  73.4 0.8 copy-start.5
  74.3 7.4 %copy-start.25 = (bf16[4,6,12,512]{3,0,2,1:T(4,128)(2,1)S(1)}, bf16[4,6,12,512]{3,0,2,1:T(4,128)(2,1)}, u32[]{:S(2)}) copy-start(bf16[4,6,12,512]{3,0,2,1:T(4,128)(2,1)} %param.19) | copy-start | bytes 884740
  74.5 8.2 %copy-start.30 = (f32[4,6,12]{0,2,1:T(8,128)S(1)}, f32[4,6,12]{0,2,1:T(8,128)}, u32[]{:S(2)}) copy-start(f32[4,6,12]{0,2,1:T(8,128)} %broadcast_multiply_fusion) | copy-start | bytes 3460
  74.5 8.4 %copy-start.31 = (pred[72,288]{1,0:T(8,128)(4,1)S(1)}, pred[72,288]{1,0:T(8,128)(4,1)}, u32[]{:S(2)}) copy-start(pred[72,288]{1,0:T(8,128)(4,1)} %broadcast_compare_fusion) | copy-start | bytes 62212
  75.5 9.4 %collective-permute-start = (bf16[4,3,12,1024]{3,2,1,0:T(8,128)(2,1)}, bf16[4,3,12,1024]{3,2,1,0:T(8,128)(2,1)S(1)}, u32[]{:S(2)}, u32[]{:S(2)}) collective-permute-start(bf16[4,3,12,1024]{3,2,1,0:T(8,128)(2,1)} %get-tuple-element.82), channel_id=1, source_target_pairs={{0,8},{8,16},{16,24},{24,32},{32,40},{40,48},{48,56},{56,64},{64,7... | collective-permute-start | bytes 884744 | tf_op jit(solution)/shard_map/ppermute | solution.py:24
  79.6 9.4 %collective-permute-start.1 = (bf16[4,3,12,1024]{3,2,1,0:T(8,128)(2,1)}, bf16[4,3,12,1024]{3,2,1,0:T(8,128)(2,1)}, u32[]{:S(2)}, u32[]{:S(2)}) collective-permute-start(bf16[4,3,12,1024]{3,2,1,0:T(8,128)(2,1)} %get-tuple-element.83), channel_id=1, source_target_pairs={{8,0},{16,8},{24,16},{32,24},{40,32},{48,40},{56,48},{64,56},{72,6... | collective-permute-start | bytes 884744 | tf_op jit(solution)/shard_map/ppermute | solution.py:25
  92.0 19.0 %collective-permute-start.2 = (bf16[4,12,6,1024]{3,0,2,1:T(4,128)(2,1)}, bf16[4,12,6,1024]{3,0,2,1:T(4,128)(2,1)}, u32[]{:S(2)}, u32[]{:S(2)}) collective-permute-start(bf16[4,12,6,1024]{3,0,2,1:T(4,128)(2,1)} %copy.102), channel_id=1, source_target_pairs={{0,1},{1,2},{2,3},{3,4},{4,5},{5,6},{6,7},{7,0},{8,9},{9,10},{10,1... | collective-permute-start | bytes 1769480 | tf_op jit(solution)/shard_map/ppermute | solution.py:24
  93.5 23.6 %collective-permute-start.3 = (bf16[4,12,6,1024]{3,0,2,1:T(4,128)(2,1)}, bf16[4,12,6,1024]{3,0,2,1:T(4,128)(2,1)}, u32[]{:S(2)}, u32[]{:S(2)}) collective-permute-start(bf16[4,12,6,1024]{3,0,2,1:T(4,128)(2,1)} %copy.103), channel_id=1, source_target_pairs={{1,0},{2,1},{3,2},{4,3},{5,4},{6,5},{7,6},{0,7},{9,8},{10,9},{11,1... | collective-permute-start | bytes 1769480 | tf_op jit(solution)/shard_map/ppermute | solution.py:25
  98.6 0.6 copy-start.34
  129.2 7.1 %copy-start.16 = (bf16[2,2,72,8,64]{2,4,3,1,0:T(8,128)(2,1)S(1)}, bf16[2,2,72,8,64]{2,4,3,1,0:T(8,128)(2,1)}, u32[]{:S(2)}) copy-start(bf16[2,2,72,8,64]{2,4,3,1,0:T(8,128)(2,1)} %copy.114) | copy-start | bytes 884740
  129.2 7.1 %copy-start.26 = (f32[2,72,288]{2,1,0:T(8,128)S(1)}, f32[2,72,288]{2,1,0:T(8,128)}, u32[]{:S(2)}) copy-start(f32[2,72,288]{2,1,0:T(8,128)} %and_convert_fusion) | copy-start | bytes 497668
  129.2 7.1 %copy-start.37 = (f32[8]{0:T(128)S(1)}, f32[8]{0:T(128)}, u32[]{:S(2)}) copy-start(f32[8]{0:T(128)} %param.18) | copy-start | bytes 100
  132.0 5.5 copy-start.1
  136.3 2.9 copy-start.3
  137.4 1.8 copy-start.12
  140.3 1.0 copy-start.11
  140.8 1.2 copy-start.7
  140.8 1.2 copy-start.36
  141.1 1.2 copy-start.22
  141.3 1.0 copy-start.15
  143.3 5.8 copy-start.4
  149.1 3.8 copy-start.13
  149.1 3.8 copy-start.20
  149.1 3.8 copy-start.27
  152.9 2.8 copy-start.17
  200.5 2.2 copy-start
  202.8 7.8 %copy-start.2 = (bf16[2,2,288,512]{2,3,1,0:T(8,128)(2,1)S(1)}, bf16[2,2,288,512]{2,3,1,0:T(8,128)(2,1)}, u32[]{:S(2)}) copy-start(bf16[2,2,288,512]{2,3,1,0:T(8,128)(2,1)} %copy-done.1) | copy-start | bytes 3538948
  204.3 41.9 %collective-permute-start.4 = (bf16[4,12,6,1024]{3,0,2,1:T(4,128)(2,1)}, bf16[4,12,6,1024]{3,0,2,1:T(4,128)(2,1)}, u32[]{:S(2)}, u32[]{:S(2)}) collective-permute-start(bf16[4,12,6,1024]{3,0,2,1:T(4,128)(2,1)} %get-tuple-element.69), channel_id=1, source_target_pairs={{7,0},{0,1},{1,2},{2,3},{3,4},{4,5},{5,6},{6,7},{15,8},{8,9},{9,10... | collective-permute-start | bytes 1769480 | tf_op jit(solution)/shard_map/ppermute | solution.py:33
  205.7 42.4 %collective-permute-start.5 = (bf16[4,12,6,1024]{3,0,2,1:T(4,128)(2,1)}, bf16[4,12,6,1024]{3,0,2,1:T(4,128)(2,1)}, u32[]{:S(2)}, u32[]{:S(2)}) collective-permute-start(bf16[4,12,6,1024]{3,0,2,1:T(4,128)(2,1)} %get-tuple-element.68), channel_id=1, source_target_pairs={{1,0},{2,1},{3,2},{4,3},{5,4},{6,5},{7,6},{0,7},{9,8},{10,9},{11,1... | collective-permute-start | bytes 1769480 | tf_op jit(solution)/shard_map/ppermute | solution.py:33
  249.7 9.2 %copy-start.14 = (f32[288,8,64]{0,2,1:T(8,128)S(1)}, f32[288,8,64]{0,2,1:T(8,128)}, u32[]{:S(2)}) copy-start(f32[288,8,64]{0,2,1:T(8,128)} %copy.125) | copy-start | bytes 1769476
  249.8 11.2 %copy-start.35 = (f32[288,8]{0,1:T(8,128)S(1)}, f32[288,8]{0,1:T(8,128)}, u32[]{:S(2)}) copy-start(f32[288,8]{0,1:T(8,128)} %copy-done.34) | copy-start | bytes 27652
  251.3 13.0 %collective-permute-start.6 = (bf16[4,3,12,1024]{3,0,2,1:T(4,128)(2,1)}, bf16[4,3,12,1024]{3,0,2,1:T(4,128)(2,1)}, u32[]{:S(2)}, u32[]{:S(2)}) collective-permute-start(bf16[4,3,12,1024]{3,0,2,1:T(4,128)(2,1)} %get-tuple-element.77), channel_id=1, source_target_pairs={{0,8},{8,16},{16,24},{24,32},{32,40},{40,48},{48,56},{56,64},{64,7... | collective-permute-start | bytes 884744 | tf_op jit(solution)/shard_map/ppermute | solution.py:39
  259.1 8.1 %collective-permute-start.7 = (bf16[4,3,12,1024]{3,0,2,1:T(4,128)(2,1)S(1)}, bf16[4,3,12,1024]{3,0,2,1:T(4,128)(2,1)}, u32[]{:S(2)}, u32[]{:S(2)}) collective-permute-start(bf16[4,3,12,1024]{3,0,2,1:T(4,128)(2,1)S(1)} %get-tuple-element.76), channel_id=1, source_target_pairs={{8,0},{16,8},{24,16},{32,24},{40,32},{48,40},{56,48},{64,56},{72,6... | collective-permute-start | bytes 884744 | tf_op jit(solution)/shard_map/ppermute | solution.py:39
  269.2 4.1 copy-start.33
  271.2 3.3 copy-start.6
  271.2 3.3 copy-start.10
  274.5 2.2 copy-start.23
  274.5 2.2 copy-start.28
  276.7 1.0 copy-start.19
  277.9 2.6 copy-start.24
  280.4 78.6 %copy-start.8 = (f32[288,512]{1,0:T(8,128)S(1)}, f32[288,512]{1,0:T(8,128)}, u32[]{:S(2)}) copy-start(f32[288,512]{1,0:T(8,128)} %reshape.465) | copy-start | bytes 1769476
  280.4 78.6 %copy-start.29 = (bf16[288,512]{1,0:T(8,128)(2,1)S(1)}, bf16[288,512]{1,0:T(8,128)(2,1)}, u32[]{:S(2)}) copy-start(bf16[288,512]{1,0:T(8,128)(2,1)} %slice.283) | copy-start | bytes 884740
  280.4 301.7 %all-reduce.2.cloned.1.call-start = ((), (), s32[]{:S(2)}) async-start(), calls=%async_computation.2 | async-start | bytes 1048576 | tf_op jit(solution)/shard_map/psum | solution.py:273
  582.1 2.1 copy-start.18
  (1 other events, 0.6 us)
Sparse Core Ops, SparseCore 0:
  10.6 59.3 all-gather.1
  280.5 76.3 reduce-scatter.3
  359.5 222.5 all-reduce.1
where the time goes:
time: 598 us; the launch traced here: 592 us
  waiting for transfers between devices  338 us (57%)
  local copies, waits for them, and re-layouts  96.4 us (16%)
  matrix products  52.7 us (9%)
  blocking collectives  34.2 us (6%)
  other arithmetic  29.8 us (5%)
  starting transfers between devices  26 us (4%)
  between operations  14.8 us (2%)
    psum x1, waiting for transfers between devices, on_device(): summed = lax.psum(shard_sum, 'lat').astype(jnp.float32)  220 us
    unnamed x4, waiting for transfers between devices  76.2 us
    all_gather x1, blocking collectives, on_device(): lax.all_gather(w_out, 'lon', axis=0, tiled=True)  34.2 us
    all_gather x1, waiting for transfers between devices, on_device(): lax.all_gather(w_qkv, 'lon', axis=0, tiled=True)  24 us
    dot_general x1, matrix products, on_device(): jnp.einsum('abhqk,abkhd->abqhd', dscore, key_u, preferred_element_type=jn...  18.4 us
    dot_general x1, matrix products, on_device(): jnp.einsum('abhqk,abqhd->abkhd', dscore, query_u, preferred_element_type=...  16.7 us
    unnamed x85, local copies, waits for them, and re-layouts  14.2 us
  transfers between devices with their start and end apart: 11, of which 7 were waited for; matrix products, arithmetic and copies ran while one was open for 10% of the time, Pallas kernels for 0%

commit v1 on v0

--- a/solution.py
+++ b/solution.py
@@ -37,6 +37,28 @@
     devices = range(lax.axis_size(axis))
     route = [(i - distance, i) for i in devices if i - distance in devices]
     return lax.ppermute(block, axis, route)
+
+
+def gather_rows(block, axis):
+    peers = lax.axis_size(axis)
+    copies = jnp.broadcast_to(block[None], (peers,) + block.shape)
+    spread = lax.all_to_all(copies, axis, 0, 0, tiled=False)
+    return spread.reshape((peers * block.shape[0],) + block.shape[1:])
+
+
+def sum_rows(partial, axis):
+    peers = lax.axis_size(axis)
+    chunks = partial.reshape((peers, partial.shape[0] // peers) + partial.shape[1:])
+    spread = lax.all_to_all(chunks, axis, 0, 0, tiled=False)
+    return jnp.sum(spread.astype(jnp.float32), axis=0)
+
+
+def sum_everywhere(partial, axis):
+    peers = lax.axis_size(axis)
+    own = sum_rows(partial, axis).astype(jnp.bfloat16)
+    copies = jnp.broadcast_to(own[None], (peers,) + own.shape)
+    spread = lax.all_to_all(copies, axis, 0, 0, tiled=False)
+    return spread.reshape((peers * own.shape[0],) + own.shape[1:])
 
 
 def unit_rows(vectors):
@@ -139,9 +161,12 @@
     tok_flat = tokens.reshape(tok_count, model_width)
     src_count = tok_flat.shape[0]
     tok_part = tok_flat
+    weights_all = gather_rows(jnp.concatenate([w_qkv, w_out], axis=1), "lon")
+    w_qkv_all = weights_all[:, : 3 * model_width]
+    w_out_all = weights_all[:, 3 * model_width :]
     projected = jnp.dot(
         tok_part,
-        lax.all_gather(w_qkv, "lon", axis=0, tiled=True),
+        w_qkv_all,
         preferred_element_type=jnp.float32,
     )
     proj_b = projected.astype(jnp.bfloat16)
@@ -197,7 +222,7 @@
     att_part = attended
     y_rows = jnp.dot(
         att_part,
-        lax.all_gather(w_out, "lon", axis=0, tiled=True),
+        w_out_all,
         preferred_element_type=jnp.float32,
     )
     normed, inverse = norm_forward(y_rows)
@@ -206,7 +231,7 @@
     grad_y = norm_back(normed, inverse, gain * cot_flat).astype(jnp.bfloat16)
     grad_att = jnp.dot(
         grad_y,
-        lax.all_gather(w_out, "lon", axis=0, tiled=True).T,
+        w_out_all.T,
         preferred_element_type=jnp.float32,
     )
     grad_att_b = grad_att.astype(jnp.bfloat16).reshape(LV, lat_rows, lon_cols, model_width)
@@ -254,7 +279,7 @@
     grad_proj = jnp.concatenate([grad_q_src, grad_k, dvalue_src], axis=1).astype(jnp.bfloat16)
     grad_in = jnp.dot(
         grad_proj,
-        lax.all_gather(w_qkv, "lon", axis=0, tiled=True).T,
+        w_qkv_all.T,
         preferred_element_type=jnp.float32,
     )
     grad_tokens = (
@@ -262,15 +287,11 @@
     )
     tok_part = tok_flat
     att_part = attended
-    shard_sum = lax.psum_scatter(
-        jnp.concatenate(
-            [cross_rows(tok_part, grad_proj), cross_rows(att_part, grad_y)], axis=1
-        ).astype(jnp.bfloat16),
-        "lon",
-        scatter_dimension=0,
-        tiled=True,
-    )
-    summed = lax.psum(shard_sum, "lat").astype(jnp.float32)
+    partial = jnp.concatenate(
+        [cross_rows(tok_part, grad_proj), cross_rows(att_part, grad_y)], axis=1
+    ).astype(jnp.bfloat16)
+    shard_sum = sum_rows(partial, "lon").astype(jnp.bfloat16)
+    summed = sum_everywhere(shard_sum, "lat").astype(jnp.float32)
     grad_qkv = summed[:, : 3 * model_width]
     grad_out = summed[:, 3 * model_width :]
     return (output.reshape(LV, lat_rows, lon_cols, model_width), grad_tokens, grad_qkv, grad_out)

time: 598 us -> 334 us (0.56)
  waiting for transfers between devices: 338 us -> 53.6 us
  blocking collectives: 34.2 us -> 52.5 us
  between operations: 14.8 us -> 2.02 us
  starting transfers between devices: 26 us -> 38.1 us
    psum x1 -> x0, waiting for transfers between devices: 220 us -> none  [on_device(): summed = lax.psum(shard_sum, 'lat').astype(jnp.float32)]
    unnamed x4 -> x0, waiting for transfers between devices: 76.2 us -> none
    all_to_all x0 -> x2, blocking collectives: none -> 52.5 us  [sum_rows(): spread = lax.all_to_all(chunks, axis, 0, 0, tiled=False)]
    all_gather x1 -> x0, blocking collectives: 34.2 us -> none  [on_device(): lax.all_gather(w_out, 'lon', axis=0, tiled=True)]
    all_to_all x0 -> x2, waiting for transfers between devices: none -> 33.4 us  [the longest x1 25.2 us: gather_rows(): spread = lax.all_to_all(copies, axis, 0, 0, tiled=False)]
    all_gather x1 -> x0, waiting for transfers between devices: 24 us -> none  [on_device(): lax.all_gather(w_qkv, 'lon', axis=0, tiled=True)]
    all_to_all x0 -> x2, starting transfers between devices: none -> 13.3 us  [the longest x1 7.61 us: gather_rows(): spread = lax.all_to_all(copies, axis, 0, 0, tiled=False)]
    unnamed x85 -> x93, local copies, waits for them, and re-layouts: 14.2 us -> 9.15 us
  transfers between devices with their start and end apart: 11 -> 10, of which waited for: 7 -> 6; matrix products, arithmetic and copies ran while one was open for 10% -> 19% of each run, Pallas kernels for 0% -> 0%
where the time goes in v1:
time: 334 us; the launch traced here: 328 us
  local copies, waits for them, and re-layouts  96.6 us (29%)
  matrix products  53.8 us (16%)
  waiting for transfers between devices  53.6 us (16%)
  blocking collectives  52.5 us (16%)
  starting transfers between devices  38.1 us (11%)
  other arithmetic  31.1 us (9%)
    all_to_all x2, blocking collectives, sum_rows(): spread = lax.all_to_all(chunks, axis, 0, 0, tiled=False)  52.5 us
    all_to_all x1, waiting for transfers between devices, gather_rows(): spread = lax.all_to_all(copies, axis, 0, 0, tiled=False)  25.2 us
    dot_general x1, matrix products, on_device(): jnp.einsum('abhqk,abkhd->abqhd', dscore, key_u, preferred_element_type=jn...  18.5 us
    dot_general x1, matrix products, on_device(): jnp.einsum('abhqk,abqhd->abkhd', dscore, query_u, preferred_element_type=...  16.7 us
    ppermute x2, waiting for transfers between devices, with_halo(): after = lax.ppermute(initial, axis, down)  11.6 us
    concatenate x2, local copies, waits for them, and re-layouts, on_device(): jnp.concatenate([dkey.reshape(row_units, col_units, KEYS, model_width), d...  9.59 us
    unnamed x93, local copies, waits for them, and re-layouts  9.15 us
    ppermute x2, starting transfers between devices, from_behind_2(): return lax.ppermute(block, axis, route)  9.09 us
  transfers between devices with their start and end apart: 10, of which 6 were waited for; matrix products, arithmetic and copies ran while one was open for 19% of the time, Pallas kernels for 0%

profile of v1, /device:TPU:1, one launch (start us, length us, event | category | flops | bytes accessed | tf_op | source)
XLA Modules:
  0.0 327.8 jit_solution(5580757708076726717)
XLA Ops:
  1.6 1.6 broadcast_in_dim.4
  3.2 7.6 %all-to-all-start = ((bf16[8,64,2048]{2,1,0:T(8,128)(2,1)}), bf16[8,64,2048]{2,1,0:T(8,128)(2,1)S(1)}, u32[]{:S(2)}, u32[]{:S(2)}) async-start(bf16[8,64,2048]{2,1,0:T(8,128)(2,1)} %broadcast_in_dim.4), calls=%async_computation | async-start | bytes 4194304 | tf_op jit(solution)/shard_map/all_to_all | solution.py:45
  13.2 25.2 %all-to-all-done = bf16[8,64,2048]{2,1,0:T(8,128)(2,1)S(1)} async-done(((bf16[8,64,2048]{2,1,0:T(8,128)(2,1)}), bf16[8,64,2048]{2,1,0:T(8,128)(2,1)S(1)}, u32[]{:S(2)}, u32[]{:S(2)}) %all-to-all-start) | async-done | bytes 2097184 | tf_op jit(solution)/shard_map/all_to_all | solution.py:45
  39.7 2.0 fusion.6
  45.2 5.3 %collective-permute-start = (bf16[4,3,12,1024]{3,2,1,0:T(8,128)(2,1)}, bf16[4,3,12,1024]{3,2,1,0:T(8,128)(2,1)S(1)}, u32[]{:S(2)}, u32[]{:S(2)}) collective-permute-start(bf16[4,3,12,1024]{3,2,1,0:T(8,128)(2,1)} %get-tuple-element.94), channel_id=1, source_target_pairs={{0,8},{8,16},{16,24},{24,32},{32,40},{40,48},{48,56},{56,64},{64,7... | collective-permute-start | bytes 884744 | tf_op jit(solution)/shard_map/ppermute | solution.py:24
  50.5 1.9 collective-permute-start.1
  56.3 3.6 %collective-permute-done.1 = bf16[4,3,12,1024]{3,2,1,0:T(8,128)(2,1)} collective-permute-done((bf16[4,3,12,1024]{3,2,1,0:T(8,128)(2,1)}, bf16[4,3,12,1024]{3,2,1,0:T(8,128)(2,1)}, u32[]{:S(2)}, u32[]{:S(2)}) %collective-permute-start.1) | collective-permute-done | bytes 294944 | tf_op jit(solution)/shard_map/ppermute | solution.py:25
  65.3 2.3 collective-permute-start.2
  73.4 8.0 %collective-permute-done.3 = bf16[4,12,6,1024]{3,0,2,1:T(4,128)(2,1)} collective-permute-done((bf16[4,12,6,1024]{3,0,2,1:T(4,128)(2,1)}, bf16[4,12,6,1024]{3,0,2,1:T(4,128)(2,1)}, u32[]{:S(2)}, u32[]{:S(2)}) %collective-permute-start.3) | collective-permute-done | bytes 589856 | tf_op jit(solution)/shard_map/ppermute | solution.py:25
  82.7 6.9 %collective-permute-done.2 = bf16[4,12,6,1024]{3,0,2,1:T(4,128)(2,1)} collective-permute-done((bf16[4,12,6,1024]{3,0,2,1:T(4,128)(2,1)}, bf16[4,12,6,1024]{3,0,2,1:T(4,128)(2,1)}, u32[]{:S(2)}, u32[]{:S(2)}) %collective-permute-start.2) | collective-permute-done | bytes 589856 | tf_op jit(solution)/shard_map/ppermute | solution.py:24
  90.8 2.3 pad_maximum_fusion
  93.1 1.8 copy.218
  98.4 3.2 pad_maximum_fusion.3
  101.6 2.8 copy.225
  104.4 4.3 %copy.221 = bf16[2,2,288,512]{2,3,1,0:T(8,128)(2,1)} copy(bf16[2,2,288,512]{3,1,2,0:T(2,128)(2,1)} %get-tuple-element.83) | data formatting | bytes 2359296 | tf_op jit(solution)/shard_map/slice | solution.py:193
  109.8 1.8 copy-done.11
  122.5 3.8 %fusion.74 = f32[2,2,8,72,288]{4,3,2,1,0:T(8,128)} fusion(bf16[2,2,72,8,64]{2,4,3,1,0:T(8,128)(2,1)} %copy.233, bf16[2,2,288,8,64]{2,4,3,1,0:T(8,128)(2,1)S(1)} %bitcast.85), kind=kOutput, calls=%fused_computation.132 | convolution fusion | flops 84934656 | bytes 4128768 | tf_op jit(solution)/shard_map/abqhd,abkhd->abhqk/dot_general | solution.py:241
  126.3 2.8 convolution_bitcast_fusion
  129.1 16.7 %fusion.13 = f32[2,2,288,8,64]{2,4,3,1,0:T(8,128)} fusion(bf16[2,2,72,8,64]{2,4,3,1,0:T(8,128)(2,1)S(1)} %copy-done.17, f32[2,2,8,72,288]{4,3,2,1,0:T(8,128)} %fusion.74, f32[8]{0:T(128)S(1)} %copy-done.42, f32[2,2,8,72,288]{4,3,2,1,0:T(8,128)} %copy-done.11, f32[2,2,8,72]{3,2,1,0:T(8,128)S(1)} %get-tuple-element.98, f32[2,72,288]{2,1,0:T(8,128)S(1)} %copy-done.29), kind=kOutput, calls=%fused_computation.18 | convolution fusion | flops 92236320 | bytes 8137760 | tf_op jit(solution)/shard_map/abhqk,abqhd->abkhd/dot_general | solution.py:245
  145.8 5.5 %copy.243 = f32[2,2,288,8,64]{4,3,1,2,0:T(8,128)} copy(f32[2,2,288,8,64]{2,4,3,1,0:T(8,128)} %convolution_bitcast_fusion) | data formatting | bytes 4718592 | tf_op jit(solution)/shard_map/abhqk,abqhd->abkhd/transpose | solution.py:246
  151.3 4.1 %concatenate.58 = f32[2,2,4,6,12,512]{5,1,4,3,2,0:T(2,128)S(1)} reshape(f32[2,2,288,8,64]{4,3,1,2,0:T(8,128)} %copy.243) | data formatting | bytes 4718592 | tf_op jit(solution)/shard_map/concatenate | solution.py:247
  155.5 5.5 %copy.241 = f32[2,2,288,8,64]{4,3,1,2,0:T(8,128)} copy(f32[2,2,288,8,64]{2,4,3,1,0:T(8,128)} %fusion.13) | data formatting | bytes 4718592 | tf_op jit(solution)/shard_map/abhqk,abqhd->abkhd/transpose | solution.py:245
  161.0 5.5 %concatenate.57 = f32[2,2,4,6,12,512]{5,1,4,3,2,0:T(2,128)} reshape(f32[2,2,288,8,64]{4,3,1,2,0:T(8,128)} %copy.241) | data formatting | bytes 4718592 | tf_op jit(solution)/shard_map/concatenate | solution.py:247
  166.5 4.3 %maximum_bitcast_fusion = f32[4,2,6,2,12,1024]{5,3,4,2,0,1:T(2,128)S(1)} fusion(f32[2,2,4,6,12,512]{5,1,4,3,2,0:T(2,128)S(1)} %concatenate.58, f32[2,2,4,6,12,512]{5,1,4,3,2,0:T(2,128)} %concatenate.57), kind=kLoop, calls=%fused_computation.1 | loop fusion | flops 1179648 | bytes 9437184 | tf_op jit(solution)/shard_map/transpose | solution.py:101
  170.8 3.1 copy.244
  176.1 1.6 fusion.68
  179.1 4.8 %collective-permute-start.5 = (bf16[4,12,6,1024]{3,0,2,1:T(4,128)(2,1)}, bf16[4,12,6,1024]{3,0,2,1:T(4,128)(2,1)}, u32[]{:S(2)}, u32[]{:S(2)}) collective-permute-start(bf16[4,12,6,1024]{3,0,2,1:T(4,128)(2,1)} %get-tuple-element.80), channel_id=1, source_target_pairs={{1,0},{2,1},{3,2},{4,3},{5,4},{6,5},{7,6},{0,7},{9,8},{10,9},{11,1... | collective-permute-start | bytes 1769480 | tf_op jit(solution)/shard_map/ppermute | solution.py:33
  183.9 18.5 %fusion.21 = f32[2,2,72,8,64]{2,4,3,1,0:T(8,128)} fusion(bf16[2,2,288,8,64]{2,4,3,1,0:T(8,128)(2,1)S(1)} %bitcast.83, f32[2,2,8,72,288]{4,3,2,1,0:T(8,128)} %fusion.74, f32[8]{0:T(128)S(1)} %copy-done.42, f32[2,2,8,72,288]{4,3,2,1,0:T(8,128)} %copy-done.11, f32[2,2,8,72]{3,2,1,0:T(8,128)S(1)} %get-tuple-element.98, f32[2,72,288]{2,1,0:T(8,128)} %and_convert_fusion), kind=kOutput, calls=%fused_computation.25 | convolution fusion | flops 92236320 | bytes 7253024 | tf_op jit(solution)/shard_map/abhqk,abkhd->abqhd/dot_general | solution.py:244
  202.4 2.6 slice.251
  205.9 2.7 copy.234
  208.6 2.6 reshape_reshape.30
  211.2 2.1 copy.235
  213.3 2.5 reshape_reshape.32
  215.8 2.6 copy.237
  218.4 2.2 convolution_convert_fusion.2
  220.6 1.9 fusion.33
  222.5 1.6 fusion.32
  225.7 7.2 %collective-permute-start.6 = (bf16[4,3,12,1024]{3,0,2,1:T(4,128)(2,1)}, bf16[4,3,12,1024]{3,0,2,1:T(4,128)(2,1)}, u32[]{:S(2)}, u32[]{:S(2)}) collective-permute-start(bf16[4,3,12,1024]{3,0,2,1:T(4,128)(2,1)} %get-tuple-element.89), channel_id=1, source_target_pairs={{0,8},{8,16},{16,24},{24,32},{32,40},{40,48},{48,56},{56,64},{64,7... | collective-permute-start | bytes 884744 | tf_op jit(solution)/shard_map/ppermute | solution.py:39
  233.0 1.9 collective-permute-start.7
  234.9 2.1 reshape_reshape.31
  239.5 1.7 collective-permute-done.7
  244.0 1.9 convert_multiply_fusion.1
  248.6 2.1 multiply_convert_fusion.2
  252.3 27.1 %all_to_all.20 = bf16[8,64,2048]{2,1,0:T(8,128)(2,1)S(1)} all-to-all(bf16[8,64,2048]{2,1,0:T(8,128)(2,1)S(1)} %pad_maximum_fusion.1), channel_id=1, replica_groups=mesh['lat'=32,'lon'=8] {'lon'}, dimensions={0} | all-to-all | bytes 4194304 | tf_op jit(solution)/shard_map/all_to_all | solution.py:52
  280.6 25.4 %all_to_all.21 = bf16[32,2,2048]{2,1,0:T(2,128)(2,1)S(1)} all-to-all(bf16[32,2,2048]{2,1,0:T(2,128)(2,1)} %reshape.480), channel_id=1, replica_groups=mesh['lat'=32,'lon'=8] {'lat'}, dimensions={0} | all-to-all | bytes 524288 | tf_op jit(solution)/shard_map/all_to_all | solution.py:52
  307.1 5.7 %all-to-all-start.3 = ((bf16[32,2,2048]{2,1,0:T(2,128)(2,1)}), bf16[32,2,2048]{2,1,0:T(2,128)(2,1)}, u32[]{:S(2)}, u32[]{:S(2)}) async-start(bf16[32,2,2048]{2,1,0:T(2,128)(2,1)} %broadcast_in_dim.5), calls=%async_computation.3 | async-start | bytes 524288 | tf_op jit(solution)/shard_map/all_to_all | solution.py:60
  313.8 1.8 fusion.28
  316.6 8.2 %all-to-all-done.3 = bf16[32,2,2048]{2,1,0:T(2,128)(2,1)} async-done(((bf16[32,2,2048]{2,1,0:T(2,128)(2,1)}), bf16[32,2,2048]{2,1,0:T(2,128)(2,1)}, u32[]{:S(2)}, u32[]{:S(2)}) %all-to-all-start.3) | async-done | bytes 262176 | tf_op jit(solution)/shard_map/all_to_all | solution.py:60
  (194 shorter events, 63.2 us)
Async XLA Ops:
  3.2 7.6 %copy-start.33 = (bf16[4,6,12,512]{3,0,2,1:T(4,128)(2,1)S(1)}, bf16[4,6,12,512]{3,0,2,1:T(4,128)(2,1)}, u32[]{:S(2)}) copy-start(bf16[4,6,12,512]{3,0,2,1:T(4,128)(2,1)} %param.14) | copy-start | bytes 884740
  3.2 8.4 %copy-start.26 = (bf16[4,6,12,512]{3,0,2,1:T(4,128)(2,1)S(1)}, bf16[4,6,12,512]{3,0,2,1:T(4,128)(2,1)}, u32[]{:S(2)}) copy-start(bf16[4,6,12,512]{3,0,2,1:T(4,128)(2,1)} %param.19) | copy-start | bytes 884740
  3.2 8.4 %copy-start.40 = (f32[512]{0:T(512)S(1)}, f32[512]{0:T(512)}, u32[]{:S(2)}) copy-start(f32[512]{0:T(512)} %param.17) | copy-start | bytes 6148
  3.2 35.1 %all-to-all-start = ((bf16[8,64,2048]{2,1,0:T(8,128)(2,1)}), bf16[8,64,2048]{2,1,0:T(8,128)(2,1)S(1)}, u32[]{:S(2)}, u32[]{:S(2)}) async-start(bf16[8,64,2048]{2,1,0:T(8,128)(2,1)} %broadcast_in_dim.4), calls=%async_computation | async-start | bytes 4194304 | tf_op jit(solution)/shard_map/all_to_all | solution.py:45
  11.0 28.7 %copy-start.21 = (bf16[288,512]{1,0:T(8,128)(2,1)}, bf16[288,512]{1,0:T(8,128)(2,1)S(1)}, u32[]{:S(2)}) copy-start(bf16[288,512]{1,0:T(8,128)(2,1)S(1)} %reshape.471) | copy-start | bytes 884740
  38.4 1.3 copy-start.13
  41.7 1.4 copy-start.9
  44.0 8.5 %copy-start.43 = (s32[2]{0:T(128)S(1)}, s32[2]{0:T(128)}, u32[]{:S(2)}) copy-start(s32[2]{0:T(128)} %fusion.57) | copy-start | bytes 28
  44.0 8.6 %copy-start.27 = (bf16[4,6,12,512]{3,0,2,1:T(4,128)(2,1)S(1)}, bf16[4,6,12,512]{3,0,2,1:T(4,128)(2,1)}, u32[]{:S(2)}) copy-start(bf16[4,6,12,512]{3,0,2,1:T(4,128)(2,1)} %param.19) | copy-start | bytes 884740
  44.1 8.6 %copy-start.34 = (f32[4,6,12]{0,2,1:T(8,128)S(1)}, f32[4,6,12]{0,2,1:T(8,128)}, u32[]{:S(2)}) copy-start(f32[4,6,12]{0,2,1:T(8,128)} %broadcast_multiply_fusion) | copy-start | bytes 3460
  44.2 10.2 %copy-start.35 = (pred[72,288]{1,0:T(8,128)(4,1)S(1)}, pred[72,288]{1,0:T(8,128)(4,1)}, u32[]{:S(2)}) copy-start(pred[72,288]{1,0:T(8,128)(4,1)} %broadcast_compare_fusion) | copy-start | bytes 62212
  45.2 11.1 %collective-permute-start = (bf16[4,3,12,1024]{3,2,1,0:T(8,128)(2,1)}, bf16[4,3,12,1024]{3,2,1,0:T(8,128)(2,1)S(1)}, u32[]{:S(2)}, u32[]{:S(2)}) collective-permute-start(bf16[4,3,12,1024]{3,2,1,0:T(8,128)(2,1)} %get-tuple-element.94), channel_id=1, source_target_pairs={{0,8},{8,16},{16,24},{24,32},{32,40},{40,48},{48,56},{56,64},{64,7... | collective-permute-start | bytes 884744 | tf_op jit(solution)/shard_map/ppermute | solution.py:24
  50.5 9.4 %collective-permute-start.1 = (bf16[4,3,12,1024]{3,2,1,0:T(8,128)(2,1)}, bf16[4,3,12,1024]{3,2,1,0:T(8,128)(2,1)}, u32[]{:S(2)}, u32[]{:S(2)}) collective-permute-start(bf16[4,3,12,1024]{3,2,1,0:T(8,128)(2,1)} %get-tuple-element.95), channel_id=1, source_target_pairs={{8,0},{16,8},{24,16},{32,24},{40,32},{48,40},{56,48},{64,56},{72,6... | collective-permute-start | bytes 884744 | tf_op jit(solution)/shard_map/ppermute | solution.py:25
  64.2 17.2 %collective-permute-start.3 = (bf16[4,12,6,1024]{3,0,2,1:T(4,128)(2,1)}, bf16[4,12,6,1024]{3,0,2,1:T(4,128)(2,1)}, u32[]{:S(2)}, u32[]{:S(2)}) collective-permute-start(bf16[4,12,6,1024]{3,0,2,1:T(4,128)(2,1)} %copy.215), channel_id=1, source_target_pairs={{1,0},{2,1},{3,2},{4,3},{5,4},{6,5},{7,6},{0,7},{9,8},{10,9},{11,1... | collective-permute-start | bytes 1769480 | tf_op jit(solution)/shard_map/ppermute | solution.py:25
  65.3 24.2 %collective-permute-start.2 = (bf16[4,12,6,1024]{3,0,2,1:T(4,128)(2,1)}, bf16[4,12,6,1024]{3,0,2,1:T(4,128)(2,1)}, u32[]{:S(2)}, u32[]{:S(2)}) collective-permute-start(bf16[4,12,6,1024]{3,0,2,1:T(4,128)(2,1)} %copy.214), channel_id=1, source_target_pairs={{0,1},{1,2},{2,3},{3,4},{4,5},{5,6},{6,7},{7,0},{8,9},{9,10},{10,1... | collective-permute-start | bytes 1769480 | tf_op jit(solution)/shard_map/ppermute | solution.py:24
  101.6 7.1 %copy-start.16 = (bf16[2,2,72,8,64]{2,4,3,1,0:T(8,128)(2,1)S(1)}, bf16[2,2,72,8,64]{2,4,3,1,0:T(8,128)(2,1)}, u32[]{:S(2)}) copy-start(bf16[2,2,72,8,64]{2,4,3,1,0:T(8,128)(2,1)} %copy.226) | copy-start | bytes 884740
  101.6 7.1 %copy-start.28 = (f32[2,72,288]{2,1,0:T(8,128)S(1)}, f32[2,72,288]{2,1,0:T(8,128)}, u32[]{:S(2)}) copy-start(f32[2,72,288]{2,1,0:T(8,128)} %and_convert_fusion) | copy-start | bytes 497668
  101.6 7.1 %copy-start.42 = (f32[8]{0:T(128)S(1)}, f32[8]{0:T(128)}, u32[]{:S(2)}) copy-start(f32[8]{0:T(128)} %param.18) | copy-start | bytes 100
  104.4 5.4 %copy-start.1 = (bf16[2,2,288,512]{2,3,1,0:T(8,128)(2,1)}, bf16[2,2,288,512]{2,3,1,0:T(8,128)(2,1)S(1)}, u32[]{:S(2)}) copy-start(bf16[2,2,288,512]{2,3,1,0:T(8,128)(2,1)S(1)} %copy.225) | copy-start | bytes 3538948
  108.7 2.9 copy-start.3
  109.8 1.8 copy-start.11
  113.2 2.2 copy-start.7
  113.5 2.2 copy-start.22
  113.5 2.2 copy-start.41
  116.7 5.8 %copy-start.4 = (bf16[2,2,288,512]{2,3,1,0:T(8,128)(2,1)S(1)}, bf16[2,2,288,512]{2,3,1,0:T(8,128)(2,1)}, u32[]{:S(2)}) copy-start(bf16[2,2,288,512]{2,3,1,0:T(8,128)(2,1)} %copy.221) | copy-start | bytes 3538948
  122.5 3.8 %copy-start.12 = (f32[2,2,8,72,288]{4,3,2,1,0:T(8,128)S(1)}, f32[2,2,8,72,288]{4,3,2,1,0:T(8,128)}, u32[]{:S(2)}) copy-start(f32[2,2,8,72,288]{4,3,2,1,0:T(8,128)} %copy-done.11) | copy-start | bytes 7962628
  122.5 3.8 %copy-start.19 = (bf16[2,2,72,8,64]{2,4,3,1,0:T(8,128)(2,1)S(1)}, bf16[2,2,72,8,64]{2,4,3,1,0:T(8,128)(2,1)}, u32[]{:S(2)}) copy-start(bf16[2,2,72,8,64]{2,4,3,1,0:T(8,128)(2,1)} %copy.233) | copy-start | bytes 884740
  122.5 3.8 %copy-start.29 = (f32[2,72,288]{2,1,0:T(8,128)S(1)}, f32[2,72,288]{2,1,0:T(8,128)}, u32[]{:S(2)}) copy-start(f32[2,72,288]{2,1,0:T(8,128)} %and_convert_fusion) | copy-start | bytes 497668
  126.3 2.8 copy-start.17
  173.9 2.2 copy-start
  176.1 7.8 %copy-start.2 = (bf16[2,2,288,512]{2,3,1,0:T(8,128)(2,1)S(1)}, bf16[2,2,288,512]{2,3,1,0:T(8,128)(2,1)}, u32[]{:S(2)}) copy-start(bf16[2,2,288,512]{2,3,1,0:T(8,128)(2,1)} %copy-done.1) | copy-start | bytes 3538948
  177.7 43.0 %collective-permute-start.4 = (bf16[4,12,6,1024]{3,0,2,1:T(4,128)(2,1)}, bf16[4,12,6,1024]{3,0,2,1:T(4,128)(2,1)}, u32[]{:S(2)}, u32[]{:S(2)}) collective-permute-start(bf16[4,12,6,1024]{3,0,2,1:T(4,128)(2,1)} %get-tuple-element.81), channel_id=1, source_target_pairs={{7,0},{0,1},{1,2},{2,3},{3,4},{4,5},{5,6},{6,7},{15,8},{8,9},{9,10... | collective-permute-start | bytes 1769480 | tf_op jit(solution)/shard_map/ppermute | solution.py:33
  179.1 43.4 %collective-permute-start.5 = (bf16[4,12,6,1024]{3,0,2,1:T(4,128)(2,1)}, bf16[4,12,6,1024]{3,0,2,1:T(4,128)(2,1)}, u32[]{:S(2)}, u32[]{:S(2)}) collective-permute-start(bf16[4,12,6,1024]{3,0,2,1:T(4,128)(2,1)} %get-tuple-element.80), channel_id=1, source_target_pairs={{1,0},{2,1},{3,2},{4,3},{5,4},{6,5},{7,6},{0,7},{9,8},{10,9},{11,1... | collective-permute-start | bytes 1769480 | tf_op jit(solution)/shard_map/ppermute | solution.py:33
  211.2 7.2 %copy-start.20 = (bf16[512,288]{1,0:T(8,128)(2,1)S(1)}, bf16[512,288]{1,0:T(8,128)(2,1)}, u32[]{:S(2)}) copy-start(bf16[512,288]{1,0:T(8,128)(2,1)} %copy.249) | copy-start | bytes 884740
  224.1 8.7 %copy-start.15 = (f32[288,8,64]{0,2,1:T(8,128)S(1)}, f32[288,8,64]{0,2,1:T(8,128)}, u32[]{:S(2)}) copy-start(f32[288,8,64]{0,2,1:T(8,128)} %copy.237) | copy-start | bytes 1769476
  224.1 10.8 %copy-start.39 = (f32[288,8]{0,1:T(8,128)S(1)}, f32[288,8]{0,1:T(8,128)}, u32[]{:S(2)}) copy-start(f32[288,8]{0,1:T(8,128)} %copy-done.38) | copy-start | bytes 27652
  225.7 12.6 %collective-permute-start.6 = (bf16[4,3,12,1024]{3,0,2,1:T(4,128)(2,1)}, bf16[4,3,12,1024]{3,0,2,1:T(4,128)(2,1)}, u32[]{:S(2)}, u32[]{:S(2)}) collective-permute-start(bf16[4,3,12,1024]{3,0,2,1:T(4,128)(2,1)} %get-tuple-element.89), channel_id=1, source_target_pairs={{0,8},{8,16},{16,24},{24,32},{32,40},{40,48},{48,56},{56,64},{64,7... | collective-permute-start | bytes 884744 | tf_op jit(solution)/shard_map/ppermute | solution.py:39
  233.0 8.1 %collective-permute-start.7 = (bf16[4,3,12,1024]{3,0,2,1:T(4,128)(2,1)S(1)}, bf16[4,3,12,1024]{3,0,2,1:T(4,128)(2,1)}, u32[]{:S(2)}, u32[]{:S(2)}) collective-permute-start(bf16[4,3,12,1024]{3,0,2,1:T(4,128)(2,1)S(1)} %get-tuple-element.88), channel_id=1, source_target_pairs={{8,0},{16,8},{24,16},{32,24},{40,32},{48,40},{56,48},{64,56},{72,6... | collective-permute-start | bytes 884744 | tf_op jit(solution)/shard_map/ppermute | solution.py:39
  243.2 4.2 %copy-start.37 = (f32[288,8]{0,1:T(8,128)S(1)}, f32[288,8]{0,1:T(8,128)}, u32[]{:S(2)}) copy-start(f32[288,8]{0,1:T(8,128)} %copy-done.36) | copy-start | bytes 27652
  245.8 2.7 copy-start.6
  245.8 2.7 copy-start.10
  248.5 2.2 copy-start.23
  248.5 2.2 copy-start.32
  250.7 1.3 copy-start.18
  279.3 33.4 %copy-start.24 = (bf16[288,512]{1,0:T(8,128)(2,1)S(1)}, bf16[288,512]{1,0:T(8,128)(2,1)}, u32[]{:S(2)}) copy-start(bf16[288,512]{1,0:T(8,128)(2,1)} %get-tuple-element.97) | copy-start | bytes 884740
  279.3 34.5 %copy-start.8 = (f32[288,512]{1,0:T(8,128)S(1)}, f32[288,512]{1,0:T(8,128)}, u32[]{:S(2)}) copy-start(f32[288,512]{1,0:T(8,128)} %reshape.483) | copy-start | bytes 1769476
  279.7 34.1 %copy-start.14 = (bf16[8,64,2048]{2,1,0:T(8,128)(2,1)S(1)}, bf16[8,64,2048]{2,1,0:T(8,128)(2,1)}, u32[]{:S(2)}) copy-start(bf16[8,64,2048]{2,1,0:T(8,128)(2,1)} %copy-done.13) | copy-start | bytes 6291460
  307.1 17.8 %all-to-all-start.3 = ((bf16[32,2,2048]{2,1,0:T(2,128)(2,1)}), bf16[32,2,2048]{2,1,0:T(2,128)(2,1)}, u32[]{:S(2)}, u32[]{:S(2)}) async-start(bf16[32,2,2048]{2,1,0:T(2,128)(2,1)} %broadcast_in_dim.5), calls=%async_computation.3 | async-start | bytes 524288 | tf_op jit(solution)/shard_map/all_to_all | solution.py:60
  (6 other events, 4.9 us)
